TPU v7x, 512 devices: a whole 4x4x16 slice. The times are simulated.
512 devices in a mesh: chan: 32 (over x_lo, z), freq: 16 (over y, x_hi, core).
Axes of the slice: x: 4 (x_hi: 2, x_lo: 2; x = x_hi * 2 + x_lo), y: 4, z: 16, core: 2. Of those that a mesh axis runs over, the one named last changes fastest.
Arguments:
- traces: bfloat16 [4096, 81920], P('chan', 'freq'), may hold values from -2000 to 2000
- kept_bins: int32 [128], replicated, may hold values from 1 to 255, as said below
- round_masks: int32 [2], replicated, may hold values from 1 to 31, as said below
Outputs:
- cross_spectra: float32 [2, 128, 2, 4096, 128], P(None, 'freq', None, 'chan')
- auto_spectra: float32 [128, 2, 4096, 128], P('freq', None, 'chan')
Inputs may be any that keep to these rules, and one draw needn't show every extreme that they name: `kept_bins`: 128 distinct bin numbers in increasing order; 1 and 255 are among them. `round_masks`: 2 distinct numbers; in round r channel block b is paired with block b XOR round_masks[r].
All inputs are finite; a program needn't handle non-finite values.
Results may differ from a plain program's by a relative error of at most 0.0066.
Values may be sent and summed in bfloat16 or wider, within the bound.
No kernel may reach another device: no remote copies, remote signals or barrier semaphores. Data moves between devices by JAX's collectives and lax.ppermute only.
A program may use at most 64 MiB of HBM per device.

v0:
```python
import math
import jax
import jax.numpy as jnp
from jax import lax
from jax.sharding import PartitionSpec as P

NS = 512
ROUNDS = 2
EPSILON = 1e-06


def shifted(block, axis, distance):
    devices = range(lax.axis_size(axis))
    route = [(i - distance, i) for i in devices if i - distance in devices]
    return lax.ppermute(block, axis, route)


def swapped(shard, axis, distance):
    return lax.ppermute(shard, axis, [(i, i ^ 1 << distance) for i in range(lax.axis_size(axis))])


def dft_table(kept_bins):
    sample_index = jnp.arange(NS, dtype=jnp.int32)
    phase_index = kept_bins[:, None] * sample_index[None, :] % NS
    angles = phase_index.astype(jnp.float32) * jnp.float32(2.0 * math.pi / NS)
    hann_taper = 0.5 - 0.5 * jnp.cos(
        sample_index.astype(jnp.float32) * jnp.float32(2.0 * math.pi / NS)
    )
    stacked = jnp.stack([hann_taper * jnp.cos(angles), -hann_taper * jnp.sin(angles)], axis=1)
    return stacked.reshape(kept_bins.shape[0] * 2, NS).astype(jnp.bfloat16)


def correlate(left_block, right_block, windows):
    products = jnp.einsum(
        "kpwc,kqwd->kpqcd", left_block, right_block, preferred_element_type=jnp.float32
    )
    real_part = products[:, 0, 0] + products[:, 1, 1]
    imag_part = products[:, 1, 0] - products[:, 0, 1]
    return jnp.stack([real_part, imag_part], axis=1) * (1.0 / math.sqrt(windows))


def body(traces, kept_bins, round_masks):
    channels, samples_here = traces.shape
    hop_length = NS // 2
    frames = samples_here // hop_length
    keep_count = kept_bins.shape[0]
    transform = dft_table(kept_bins)
    following = shifted(traces[:, :hop_length], "freq", -1)
    extended = jnp.concatenate([traces, following], axis=1).reshape(
        channels, frames + 1, hop_length
    )
    spectra = jnp.einsum(
        "kn,cjn->kjc",
        transform[:, :hop_length],
        extended[:, :-1],
        preferred_element_type=jnp.float32,
    )
    spectra = spectra + jnp.einsum(
        "kn,cjn->kjc",
        transform[:, hop_length:],
        extended[:, 1:],
        preferred_element_type=jnp.float32,
    )
    rounded = spectra.astype(jnp.bfloat16).reshape(keep_count, 2, frames * channels)
    windows = frames * lax.axis_size("freq")
    values = rounded.astype(jnp.float32).reshape(keep_count, 2, frames, channels)
    partial_power = jnp.sum(values * values, axis=(1, 2))
    power_mean = lax.psum(partial_power, "freq") / windows
    whitened = (values * lax.rsqrt(power_mean + EPSILON)[:, None, None, :]).astype(jnp.bfloat16)
    arrived_bins = lax.all_to_all(
        whitened.reshape(keep_count, 2, frames * channels),
        "freq",
        split_axis=0,
        concat_axis=2,
        tiled=True,
    )
    own_block = arrived_bins.reshape(-1, 2, windows, channels)
    auto_spectra = correlate(own_block, own_block, windows)
    blocks_count = lax.axis_size("chan")
    crosses = []
    levels = blocks_count.bit_length() - 1
    for round_no in range(ROUNDS):
        round_mask = round_masks[round_no]
        carried = own_block
        for which_bit in range(levels):
            arrived = swapped(carried, "chan", which_bit)
            chosen = jnp.bitwise_and(jnp.right_shift(round_mask, which_bit), 1) == 1
            carried = jnp.where(chosen, arrived, carried)
        crosses.append(correlate(own_block, carried, windows))
    return (jnp.stack(crosses), auto_spectra)


def solution(mesh):
    placed = (P("chan", "freq"), P(), P())
    return jax.shard_map(
        body,
        mesh=mesh,
        in_specs=placed,
        out_specs=(P(None, "freq", None, "chan", None), P("freq", None, "chan", None)),
        check_vma=False,
    )
```

profile of v0, /device:TPU:8, one launch (start us, length us, event | category | flops | bytes accessed | tf_op | source)
XLA Modules:
  0.0 897.9 jit_solution(6204677982949660020)
XLA Ops:
  9.0 4.3 collective-permute-start
  19.2 2.4 copy.77
  21.6 2.5 reshape.423
  24.1 141.0 %all-reduce.2.cloned.1.call-done = f32[128,128]{1,0:T(8,128)} async-done(((f32[128,128]{1,0:T(8,128)}), f32[128,128]{1,0:T(8,128)}) %all-reduce.2.cloned.1.call-update) | async-done | bytes 65552 | tf_op jit(solution)/shard_map/psum | solution.py:68
  167.3 2.9 copy.80
  170.2 2.7 multiply_convert_fusion
  172.9 24.6 %all_to_all.15 = bf16[128,2,2560]{2,1,0:T(2,128)(2,1)S(1)} all-to-all(bf16[128,2,2560]{2,1,0:T(2,128)(2,1)S(1)} %multiply_convert_fusion), channel_id=1, replica_groups=mesh['chan'=32,'freq'=16] {'freq'}, dimensions={0} | all-to-all | bytes 2621440 | tf_op jit(solution)/shard_map/all_to_all | solution.py:70
  199.9 3.3 collective-permute-start.1
  205.1 28.3 %collective-permute-done.1 = bf16[8,2,320,128]{3,2,1,0:T(8,128)(2,1)S(1)} collective-permute-done((bf16[8,2,320,128]{3,2,1,0:T(8,128)(2,1)S(1)}, bf16[8,2,320,128]{3,2,1,0:T(8,128)(2,1)S(1)}, u32[]{:S(2)}, u32[]{:S(2)}) %collective-permute-start.1) | collective-permute-done | bytes 1310752 | tf_op jit(solution)/shard_map/ppermute | solution.py:19
  233.5 4.2 collective-permute-start.2
  237.7 2.6 collective-permute-start.6
  240.9 83.0 %collective-permute-done.2 = bf16[8,2,320,128]{3,2,1,0:T(8,128)(2,1)S(1)} collective-permute-done((bf16[8,2,320,128]{3,2,1,0:T(8,128)(2,1)S(1)}, bf16[8,2,320,128]{3,2,1,0:T(8,128)(2,1)S(1)}, u32[]{:S(2)}, u32[]{:S(2)}) %collective-permute-start.2) | collective-permute-done | bytes 1310752 | tf_op jit(solution)/shard_map/ppermute | solution.py:19
  324.1 7.6 collective-permute-start.3
  332.3 22.4 %collective-permute-done.6 = bf16[8,2,320,128]{3,2,1,0:T(8,128)(2,1)S(1)} collective-permute-done((bf16[8,2,320,128]{3,2,1,0:T(8,128)(2,1)S(1)}, bf16[8,2,320,128]{3,2,1,0:T(8,128)(2,1)S(1)}, u32[]{:S(2)}, u32[]{:S(2)}) %collective-permute-start.6) | collective-permute-done | bytes 1310752 | tf_op jit(solution)/shard_map/ppermute | solution.py:19
  354.9 33.1 %collective-permute-start.7 = (bf16[8,2,320,128]{3,2,1,0:T(8,128)(2,1)S(1)}, bf16[8,2,320,128]{3,2,1,0:T(8,128)(2,1)S(1)}, u32[]{:S(2)}, u32[]{:S(2)}) collective-permute-start(bf16[8,2,320,128]{3,2,1,0:T(8,128)(2,1)S(1)} %broadcast_select_fusion.1), channel_id=1, source_target_pairs={{0,64},{16,80},{32,96},{48,112},{64,0},{80,16},{96,32},{112,48},{1... | collective-permute-start | bytes 3932168 | tf_op jit(solution)/shard_map/ppermute | solution.py:19
  388.6 226.2 %collective-permute-done.3 = bf16[8,2,320,128]{3,2,1,0:T(8,128)(2,1)S(1)} collective-permute-done((bf16[8,2,320,128]{3,2,1,0:T(8,128)(2,1)S(1)}, bf16[8,2,320,128]{3,2,1,0:T(8,128)(2,1)S(1)}, u32[]{:S(2)}, u32[]{:S(2)}) %collective-permute-start.3) | collective-permute-done | bytes 1310752 | tf_op jit(solution)/shard_map/ppermute | solution.py:19
  614.9 10.5 %collective-permute-start.4 = (bf16[8,2,320,128]{3,2,1,0:T(8,128)(2,1)S(1)}, bf16[8,2,320,128]{3,2,1,0:T(8,128)(2,1)S(1)}, u32[]{:S(2)}, u32[]{:S(2)}) collective-permute-start(bf16[8,2,320,128]{3,2,1,0:T(8,128)(2,1)S(1)} %broadcast_select_fusion.6), channel_id=1, source_target_pairs={{0,128},{16,144},{32,160},{48,176},{64,192},{80,208},{96,224},{112... | collective-permute-start | bytes 3932168 | tf_op jit(solution)/shard_map/ppermute | solution.py:19
  626.1 43.4 %collective-permute-done.7 = bf16[8,2,320,128]{3,2,1,0:T(8,128)(2,1)S(1)} collective-permute-done((bf16[8,2,320,128]{3,2,1,0:T(8,128)(2,1)S(1)}, bf16[8,2,320,128]{3,2,1,0:T(8,128)(2,1)S(1)}, u32[]{:S(2)}, u32[]{:S(2)}) %collective-permute-start.7) | collective-permute-done | bytes 1310752 | tf_op jit(solution)/shard_map/ppermute | solution.py:19
  670.7 123.7 %collective-permute-start.8 = (bf16[8,2,320,128]{3,2,1,0:T(8,128)(2,1)}, bf16[8,2,320,128]{3,2,1,0:T(8,128)(2,1)}, u32[]{:S(2)}, u32[]{:S(2)}) collective-permute-start(bf16[8,2,320,128]{3,2,1,0:T(8,128)(2,1)} %broadcast_select_fusion.2), channel_id=1, source_target_pairs={{0,128},{16,144},{32,160},{48,176},{64,192},{80,208},{96,224},{112... | collective-permute-start | bytes 3932168 | tf_op jit(solution)/shard_map/ppermute | solution.py:19
  796.3 2.9 collective-permute-start.5
  803.5 48.4 %collective-permute-done.8 = bf16[8,2,320,128]{3,2,1,0:T(8,128)(2,1)} collective-permute-done((bf16[8,2,320,128]{3,2,1,0:T(8,128)(2,1)}, bf16[8,2,320,128]{3,2,1,0:T(8,128)(2,1)}, u32[]{:S(2)}, u32[]{:S(2)}) %collective-permute-start.8) | collective-permute-done | bytes 1310752 | tf_op jit(solution)/shard_map/ppermute | solution.py:19
  851.9 2.5 broadcast_select_fusion.3
  854.4 2.7 collective-permute-start.9
  860.9 25.6 %collective-permute-done.9 = bf16[8,2,320,128]{3,2,1,0:T(8,128)(2,1)} collective-permute-done((bf16[8,2,320,128]{3,2,1,0:T(8,128)(2,1)}, bf16[8,2,320,128]{3,2,1,0:T(8,128)(2,1)}, u32[]{:S(2)}, u32[]{:S(2)}) %collective-permute-start.9) | collective-permute-done | bytes 1310752 | tf_op jit(solution)/shard_map/ppermute | solution.py:19
  (51 shorter events, 26.4 us)
Async XLA Ops:
  7.2 6.2 copy-start.2
  7.2 158.0 %all-reduce.2.cloned.1.call-start = ((), (), s32[]{:S(2)}) async-start(), calls=%async_computation.1 | async-start | bytes 131072 | tf_op jit(solution)/shard_map/psum | solution.py:68
  9.0 6.1 collective-permute-start
  167.3 2.9 copy-start
  198.3 4.9 copy-start.1
  199.9 33.5 %collective-permute-start.1 = (bf16[8,2,320,128]{3,2,1,0:T(8,128)(2,1)S(1)}, bf16[8,2,320,128]{3,2,1,0:T(8,128)(2,1)S(1)}, u32[]{:S(2)}, u32[]{:S(2)}) collective-permute-start(bf16[8,2,320,128]{3,2,1,0:T(8,128)(2,1)S(1)} %reshape.422), channel_id=1, source_target_pairs={{0,16},{16,0},{32,48},{48,32},{64,80},{80,64},{96,112},{112,96},{1... | collective-permute-start | bytes 3932168 | tf_op jit(solution)/shard_map/ppermute | solution.py:19
  233.5 90.4 %collective-permute-start.2 = (bf16[8,2,320,128]{3,2,1,0:T(8,128)(2,1)S(1)}, bf16[8,2,320,128]{3,2,1,0:T(8,128)(2,1)S(1)}, u32[]{:S(2)}, u32[]{:S(2)}) collective-permute-start(bf16[8,2,320,128]{3,2,1,0:T(8,128)(2,1)S(1)} %get-tuple-element.14), channel_id=1, source_target_pairs={{0,32},{16,48},{32,0},{48,16},{64,96},{80,112},{96,64},{112,80},{1... | collective-permute-start | bytes 3932168 | tf_op jit(solution)/shard_map/ppermute | solution.py:19
  237.7 117.0 %collective-permute-start.6 = (bf16[8,2,320,128]{3,2,1,0:T(8,128)(2,1)S(1)}, bf16[8,2,320,128]{3,2,1,0:T(8,128)(2,1)S(1)}, u32[]{:S(2)}, u32[]{:S(2)}) collective-permute-start(bf16[8,2,320,128]{3,2,1,0:T(8,128)(2,1)S(1)} %get-tuple-element.15), channel_id=1, source_target_pairs={{0,32},{16,48},{32,0},{48,16},{64,96},{80,112},{96,64},{112,80},{1... | collective-permute-start | bytes 3932168 | tf_op jit(solution)/shard_map/ppermute | solution.py:19
  324.1 290.7 %collective-permute-start.3 = (bf16[8,2,320,128]{3,2,1,0:T(8,128)(2,1)S(1)}, bf16[8,2,320,128]{3,2,1,0:T(8,128)(2,1)S(1)}, u32[]{:S(2)}, u32[]{:S(2)}) collective-permute-start(bf16[8,2,320,128]{3,2,1,0:T(8,128)(2,1)S(1)} %broadcast_select_fusion.5), channel_id=1, source_target_pairs={{0,64},{16,80},{32,96},{48,112},{64,0},{80,16},{96,32},{112,48},{1... | collective-permute-start | bytes 3932168 | tf_op jit(solution)/shard_map/ppermute | solution.py:19
  354.9 314.6 %collective-permute-start.7 = (bf16[8,2,320,128]{3,2,1,0:T(8,128)(2,1)S(1)}, bf16[8,2,320,128]{3,2,1,0:T(8,128)(2,1)S(1)}, u32[]{:S(2)}, u32[]{:S(2)}) collective-permute-start(bf16[8,2,320,128]{3,2,1,0:T(8,128)(2,1)S(1)} %broadcast_select_fusion.1), channel_id=1, source_target_pairs={{0,64},{16,80},{32,96},{48,112},{64,0},{80,16},{96,32},{112,48},{1... | collective-permute-start | bytes 3932168 | tf_op jit(solution)/shard_map/ppermute | solution.py:19
  614.9 180.1 %collective-permute-start.4 = (bf16[8,2,320,128]{3,2,1,0:T(8,128)(2,1)S(1)}, bf16[8,2,320,128]{3,2,1,0:T(8,128)(2,1)S(1)}, u32[]{:S(2)}, u32[]{:S(2)}) collective-permute-start(bf16[8,2,320,128]{3,2,1,0:T(8,128)(2,1)S(1)} %broadcast_select_fusion.6), channel_id=1, source_target_pairs={{0,128},{16,144},{32,160},{48,176},{64,192},{80,208},{96,224},{112... | collective-permute-start | bytes 3932168 | tf_op jit(solution)/shard_map/ppermute | solution.py:19
  670.7 181.2 %collective-permute-start.8 = (bf16[8,2,320,128]{3,2,1,0:T(8,128)(2,1)}, bf16[8,2,320,128]{3,2,1,0:T(8,128)(2,1)}, u32[]{:S(2)}, u32[]{:S(2)}) collective-permute-start(bf16[8,2,320,128]{3,2,1,0:T(8,128)(2,1)} %broadcast_select_fusion.2), channel_id=1, source_target_pairs={{0,128},{16,144},{32,160},{48,176},{64,192},{80,208},{96,224},{112... | collective-permute-start | bytes 3932168 | tf_op jit(solution)/shard_map/ppermute | solution.py:19
  796.3 62.4 %collective-permute-start.5 = (bf16[8,2,320,128]{3,2,1,0:T(8,128)(2,1)}, bf16[8,2,320,128]{3,2,1,0:T(8,128)(2,1)}, u32[]{:S(2)}, u32[]{:S(2)}) collective-permute-start(bf16[8,2,320,128]{3,2,1,0:T(8,128)(2,1)} %broadcast_select_fusion.7), channel_id=1, source_target_pairs={{0,256},{16,272},{32,288},{48,304},{64,320},{80,336},{96,352},{112... | collective-permute-start | bytes 3932168 | tf_op jit(solution)/shard_map/ppermute | solution.py:19
  854.4 32.1 %collective-permute-start.9 = (bf16[8,2,320,128]{3,2,1,0:T(8,128)(2,1)}, bf16[8,2,320,128]{3,2,1,0:T(8,128)(2,1)}, u32[]{:S(2)}, u32[]{:S(2)}) collective-permute-start(bf16[8,2,320,128]{3,2,1,0:T(8,128)(2,1)} %broadcast_select_fusion.3), channel_id=1, source_target_pairs={{0,256},{16,272},{32,288},{48,304},{64,320},{80,336},{96,352},{112... | collective-permute-start | bytes 3932168 | tf_op jit(solution)/shard_map/ppermute | solution.py:19
Sparse Core Ops, SparseCore 0:
  17.5 147.5 all-reduce.1
where the time goes:
time: 899 us; the launch traced here: 898 us
  waiting for transfers between devices  618 us (69%)
  starting transfers between devices  195 us (22%)
  blocking collectives  24.6 us (3%)
  between operations  20.8 us (2%)
  local copies, waits for them, and re-layouts  19.1 us (2%)
  other arithmetic  13.9 us (2%)
    ppermute x9, waiting for transfers between devices, swapped(): lax.ppermute(shard, axis, [(i, i ^ 1 << distance) for i in range(lax.axis...  477 us
    ppermute x9, starting transfers between devices, swapped(): lax.ppermute(shard, axis, [(i, i ^ 1 << distance) for i in range(lax.axis...  190 us
    psum x1, waiting for transfers between devices, body(): power_mean = lax.psum(partial_power, 'freq') / windows  141 us
    all_to_all x1, blocking collectives, body(): lax.all_to_all(whitened.reshape(keep_count, 2, frames * channels), 'freq'...  24.6 us
  transfers between devices with their start and end apart: 11, of which 9 were waited for; matrix products, arithmetic and copies ran while one was open for 2% of the time, Pallas kernels for 0%

commit v1 on v0

--- a/solution.py
+++ b/solution.py
@@ -65,7 +65,7 @@
     windows = frames * lax.axis_size("freq")
     values = rounded.astype(jnp.float32).reshape(keep_count, 2, frames, channels)
     partial_power = jnp.sum(values * values, axis=(1, 2))
-    power_mean = lax.psum(partial_power, "freq") / windows
+    power_mean = jnp.sum(lax.all_gather(partial_power, "freq"), axis=0) / windows
     whitened = (values * lax.rsqrt(power_mean + EPSILON)[:, None, None, :]).astype(jnp.bfloat16)
     arrived_bins = lax.all_to_all(
         whitened.reshape(keep_count, 2, frames * channels),

time: 899 us -> 815 us (0.907)
  the two profiles are of different devices: /device:TPU:8 before, /device:TPU:10 now
where the time goes in v1:
time: 815 us; the launch traced here: 814 us
  waiting for transfers between devices  536 us (66%)
  starting transfers between devices  194 us (24%)
  blocking collectives  23.4 us (3%)
  between operations  20.8 us (3%)
  local copies, waits for them, and re-layouts  19.1 us (2%)
  other arithmetic  14.4 us (2%)
    ppermute x9, waiting for transfers between devices, swapped(): lax.ppermute(shard, axis, [(i, i ^ 1 << distance) for i in range(lax.axis...  477 us
    ppermute x9, starting transfers between devices, swapped(): lax.ppermute(shard, axis, [(i, i ^ 1 << distance) for i in range(lax.axis...  191 us
    all_gather x1, waiting for transfers between devices, body(): lax.all_gather(partial_power, 'freq')  58.8 us
    all_to_all x1, blocking collectives, body(): lax.all_to_all(whitened.reshape(keep_count, 2, frames * channels), 'freq'...  23.4 us
  transfers between devices with their start and end apart: 11, of which 9 were waited for; matrix products, arithmetic and copies ran while one was open for 3% of the time, Pallas kernels for 0%

profile of v1, /device:TPU:10, one launch (start us, length us, event | category | flops | bytes accessed | tf_op | source)
XLA Modules:
  0.0 814.3 jit_solution(2783745657284500279)
XLA Ops:
  9.0 3.4 collective-permute-start
  18.3 2.4 copy.92
  20.7 2.5 reshape.427
  23.2 58.8 %all-gather.3.cloned.1.call-done = f32[2048,128]{1,0:T(8,128)} async-done(((f32[128,128]{1,0:T(8,128)}), f32[2048,128]{1,0:T(8,128)}) %all-gather.3.cloned.1.call-update) | async-done | bytes 1048592 | tf_op jit(solution)/shard_map/all_gather | solution.py:68
  84.7 2.9 copy.95
  87.6 2.7 multiply_convert_fusion
  90.3 23.4 %all_to_all.15 = bf16[128,2,2560]{2,1,0:T(2,128)(2,1)S(1)} all-to-all(bf16[128,2,2560]{2,1,0:T(2,128)(2,1)S(1)} %multiply_convert_fusion), channel_id=1, replica_groups=mesh['chan'=32,'freq'=16] {'freq'}, dimensions={0} | all-to-all | bytes 2621440 | tf_op jit(solution)/shard_map/all_to_all | solution.py:70
  116.1 3.5 collective-permute-start.1
  121.4 28.0 %collective-permute-done.1 = bf16[8,2,320,128]{3,2,1,0:T(8,128)(2,1)S(1)} collective-permute-done((bf16[8,2,320,128]{3,2,1,0:T(8,128)(2,1)S(1)}, bf16[8,2,320,128]{3,2,1,0:T(8,128)(2,1)S(1)}, u32[]{:S(2)}, u32[]{:S(2)}) %collective-permute-start.1) | collective-permute-done | bytes 1310752 | tf_op jit(solution)/shard_map/ppermute | solution.py:19
  149.6 4.5 collective-permute-start.2
  154.1 2.3 collective-permute-start.6
  157.0 83.2 %collective-permute-done.2 = bf16[8,2,320,128]{3,2,1,0:T(8,128)(2,1)S(1)} collective-permute-done((bf16[8,2,320,128]{3,2,1,0:T(8,128)(2,1)S(1)}, bf16[8,2,320,128]{3,2,1,0:T(8,128)(2,1)S(1)}, u32[]{:S(2)}, u32[]{:S(2)}) %collective-permute-start.2) | collective-permute-done | bytes 1310752 | tf_op jit(solution)/shard_map/ppermute | solution.py:19
  240.4 7.6 collective-permute-start.3
  248.7 22.6 %collective-permute-done.6 = bf16[8,2,320,128]{3,2,1,0:T(8,128)(2,1)S(1)} collective-permute-done((bf16[8,2,320,128]{3,2,1,0:T(8,128)(2,1)S(1)}, bf16[8,2,320,128]{3,2,1,0:T(8,128)(2,1)S(1)}, u32[]{:S(2)}, u32[]{:S(2)}) %collective-permute-start.6) | collective-permute-done | bytes 1310752 | tf_op jit(solution)/shard_map/ppermute | solution.py:19
  271.4 32.9 %collective-permute-start.7 = (bf16[8,2,320,128]{3,2,1,0:T(8,128)(2,1)S(1)}, bf16[8,2,320,128]{3,2,1,0:T(8,128)(2,1)S(1)}, u32[]{:S(2)}, u32[]{:S(2)}) collective-permute-start(bf16[8,2,320,128]{3,2,1,0:T(8,128)(2,1)S(1)} %broadcast_select_fusion.1), channel_id=1, source_target_pairs={{0,64},{16,80},{32,96},{48,112},{64,0},{80,16},{96,32},{112,48},{1... | collective-permute-start | bytes 3932168 | tf_op jit(solution)/shard_map/ppermute | solution.py:19
  304.9 225.9 %collective-permute-done.3 = bf16[8,2,320,128]{3,2,1,0:T(8,128)(2,1)S(1)} collective-permute-done((bf16[8,2,320,128]{3,2,1,0:T(8,128)(2,1)S(1)}, bf16[8,2,320,128]{3,2,1,0:T(8,128)(2,1)S(1)}, u32[]{:S(2)}, u32[]{:S(2)}) %collective-permute-start.3) | collective-permute-done | bytes 1310752 | tf_op jit(solution)/shard_map/ppermute | solution.py:19
  531.0 10.8 %collective-permute-start.4 = (bf16[8,2,320,128]{3,2,1,0:T(8,128)(2,1)S(1)}, bf16[8,2,320,128]{3,2,1,0:T(8,128)(2,1)S(1)}, u32[]{:S(2)}, u32[]{:S(2)}) collective-permute-start(bf16[8,2,320,128]{3,2,1,0:T(8,128)(2,1)S(1)} %broadcast_select_fusion.6), channel_id=1, source_target_pairs={{0,128},{16,144},{32,160},{48,176},{64,192},{80,208},{96,224},{112... | collective-permute-start | bytes 3932168 | tf_op jit(solution)/shard_map/ppermute | solution.py:19
  542.4 42.9 %collective-permute-done.7 = bf16[8,2,320,128]{3,2,1,0:T(8,128)(2,1)S(1)} collective-permute-done((bf16[8,2,320,128]{3,2,1,0:T(8,128)(2,1)S(1)}, bf16[8,2,320,128]{3,2,1,0:T(8,128)(2,1)S(1)}, u32[]{:S(2)}, u32[]{:S(2)}) %collective-permute-start.7) | collective-permute-done | bytes 1310752 | tf_op jit(solution)/shard_map/ppermute | solution.py:19
  586.5 124.2 %collective-permute-start.8 = (bf16[8,2,320,128]{3,2,1,0:T(8,128)(2,1)}, bf16[8,2,320,128]{3,2,1,0:T(8,128)(2,1)}, u32[]{:S(2)}, u32[]{:S(2)}) collective-permute-start(bf16[8,2,320,128]{3,2,1,0:T(8,128)(2,1)} %broadcast_select_fusion.2), channel_id=1, source_target_pairs={{0,128},{16,144},{32,160},{48,176},{64,192},{80,208},{96,224},{112... | collective-permute-start | bytes 3932168 | tf_op jit(solution)/shard_map/ppermute | solution.py:19
  712.6 2.6 collective-permute-start.5
  719.6 48.7 %collective-permute-done.8 = bf16[8,2,320,128]{3,2,1,0:T(8,128)(2,1)} collective-permute-done((bf16[8,2,320,128]{3,2,1,0:T(8,128)(2,1)}, bf16[8,2,320,128]{3,2,1,0:T(8,128)(2,1)}, u32[]{:S(2)}, u32[]{:S(2)}) %collective-permute-start.8) | collective-permute-done | bytes 1310752 | tf_op jit(solution)/shard_map/ppermute | solution.py:19
  768.2 2.5 broadcast_select_fusion.3
  770.7 2.4 collective-permute-start.9
  777.0 25.9 %collective-permute-done.9 = bf16[8,2,320,128]{3,2,1,0:T(8,128)(2,1)} collective-permute-done((bf16[8,2,320,128]{3,2,1,0:T(8,128)(2,1)}, bf16[8,2,320,128]{3,2,1,0:T(8,128)(2,1)}, u32[]{:S(2)}, u32[]{:S(2)}) %collective-permute-start.9) | collective-permute-done | bytes 1310752 | tf_op jit(solution)/shard_map/ppermute | solution.py:19
  (52 shorter events, 26.9 us)
Async XLA Ops:
  7.2 5.3 copy-start.2
  7.2 74.9 %all-gather.3.cloned.1.call-start = ((), (), s32[]{:S(2)}) async-start(), calls=%async_computation.1 | async-start | bytes 1114112 | tf_op jit(solution)/shard_map/all_gather | solution.py:68
  9.0 5.2 collective-permute-start
  84.7 2.9 copy-start
  114.4 5.1 copy-start.1
  116.1 33.4 %collective-permute-start.1 = (bf16[8,2,320,128]{3,2,1,0:T(8,128)(2,1)S(1)}, bf16[8,2,320,128]{3,2,1,0:T(8,128)(2,1)S(1)}, u32[]{:S(2)}, u32[]{:S(2)}) collective-permute-start(bf16[8,2,320,128]{3,2,1,0:T(8,128)(2,1)S(1)} %reshape.426), channel_id=1, source_target_pairs={{0,16},{16,0},{32,48},{48,32},{64,80},{80,64},{96,112},{112,96},{1... | collective-permute-start | bytes 3932168 | tf_op jit(solution)/shard_map/ppermute | solution.py:19
  149.6 90.6 %collective-permute-start.2 = (bf16[8,2,320,128]{3,2,1,0:T(8,128)(2,1)S(1)}, bf16[8,2,320,128]{3,2,1,0:T(8,128)(2,1)S(1)}, u32[]{:S(2)}, u32[]{:S(2)}) collective-permute-start(bf16[8,2,320,128]{3,2,1,0:T(8,128)(2,1)S(1)} %get-tuple-element.16), channel_id=1, source_target_pairs={{0,32},{16,48},{32,0},{48,16},{64,96},{80,112},{96,64},{112,80},{1... | collective-permute-start | bytes 3932168 | tf_op jit(solution)/shard_map/ppermute | solution.py:19
  154.1 117.2 %collective-permute-start.6 = (bf16[8,2,320,128]{3,2,1,0:T(8,128)(2,1)S(1)}, bf16[8,2,320,128]{3,2,1,0:T(8,128)(2,1)S(1)}, u32[]{:S(2)}, u32[]{:S(2)}) collective-permute-start(bf16[8,2,320,128]{3,2,1,0:T(8,128)(2,1)S(1)} %get-tuple-element.17), channel_id=1, source_target_pairs={{0,32},{16,48},{32,0},{48,16},{64,96},{80,112},{96,64},{112,80},{1... | collective-permute-start | bytes 3932168 | tf_op jit(solution)/shard_map/ppermute | solution.py:19
  240.4 290.5 %collective-permute-start.3 = (bf16[8,2,320,128]{3,2,1,0:T(8,128)(2,1)S(1)}, bf16[8,2,320,128]{3,2,1,0:T(8,128)(2,1)S(1)}, u32[]{:S(2)}, u32[]{:S(2)}) collective-permute-start(bf16[8,2,320,128]{3,2,1,0:T(8,128)(2,1)S(1)} %broadcast_select_fusion.5), channel_id=1, source_target_pairs={{0,64},{16,80},{32,96},{48,112},{64,0},{80,16},{96,32},{112,48},{1... | collective-permute-start | bytes 3932168 | tf_op jit(solution)/shard_map/ppermute | solution.py:19
  271.4 313.9 %collective-permute-start.7 = (bf16[8,2,320,128]{3,2,1,0:T(8,128)(2,1)S(1)}, bf16[8,2,320,128]{3,2,1,0:T(8,128)(2,1)S(1)}, u32[]{:S(2)}, u32[]{:S(2)}) collective-permute-start(bf16[8,2,320,128]{3,2,1,0:T(8,128)(2,1)S(1)} %broadcast_select_fusion.1), channel_id=1, source_target_pairs={{0,64},{16,80},{32,96},{48,112},{64,0},{80,16},{96,32},{112,48},{1... | collective-permute-start | bytes 3932168 | tf_op jit(solution)/shard_map/ppermute | solution.py:19
  531.0 180.4 %collective-permute-start.4 = (bf16[8,2,320,128]{3,2,1,0:T(8,128)(2,1)S(1)}, bf16[8,2,320,128]{3,2,1,0:T(8,128)(2,1)S(1)}, u32[]{:S(2)}, u32[]{:S(2)}) collective-permute-start(bf16[8,2,320,128]{3,2,1,0:T(8,128)(2,1)S(1)} %broadcast_select_fusion.6), channel_id=1, source_target_pairs={{0,128},{16,144},{32,160},{48,176},{64,192},{80,208},{96,224},{112... | collective-permute-start | bytes 3932168 | tf_op jit(solution)/shard_map/ppermute | solution.py:19
  586.5 181.7 %collective-permute-start.8 = (bf16[8,2,320,128]{3,2,1,0:T(8,128)(2,1)}, bf16[8,2,320,128]{3,2,1,0:T(8,128)(2,1)}, u32[]{:S(2)}, u32[]{:S(2)}) collective-permute-start(bf16[8,2,320,128]{3,2,1,0:T(8,128)(2,1)} %broadcast_select_fusion.2), channel_id=1, source_target_pairs={{0,128},{16,144},{32,160},{48,176},{64,192},{80,208},{96,224},{112... | collective-permute-start | bytes 3932168 | tf_op jit(solution)/shard_map/ppermute | solution.py:19
  712.6 62.1 %collective-permute-start.5 = (bf16[8,2,320,128]{3,2,1,0:T(8,128)(2,1)}, bf16[8,2,320,128]{3,2,1,0:T(8,128)(2,1)}, u32[]{:S(2)}, u32[]{:S(2)}) collective-permute-start(bf16[8,2,320,128]{3,2,1,0:T(8,128)(2,1)} %broadcast_select_fusion.7), channel_id=1, source_target_pairs={{0,256},{16,272},{32,288},{48,304},{64,320},{80,336},{96,352},{112... | collective-permute-start | bytes 3932168 | tf_op jit(solution)/shard_map/ppermute | solution.py:19
  770.7 32.1 %collective-permute-start.9 = (bf16[8,2,320,128]{3,2,1,0:T(8,128)(2,1)}, bf16[8,2,320,128]{3,2,1,0:T(8,128)(2,1)}, u32[]{:S(2)}, u32[]{:S(2)}) collective-permute-start(bf16[8,2,320,128]{3,2,1,0:T(8,128)(2,1)} %broadcast_select_fusion.3), channel_id=1, source_target_pairs={{0,256},{16,272},{32,288},{48,304},{64,320},{80,336},{96,352},{112... | collective-permute-start | bytes 3932168 | tf_op jit(solution)/shard_map/ppermute | solution.py:19
Sparse Core Ops, SparseCore 0:
  16.6 65.4 all-gather.2
